TPU v7x, 32 devices: a whole 2x2x4 slice. The times are simulated.
32 devices in a mesh: dp: 8 (over z, core), mask: 4 (over y, x).
Axes of the slice: x: 2, y: 2, z: 4, core: 2. Of those that a mesh axis runs over, the one named last changes fastest.
Arguments:
- patches: bfloat16 [2048, 768], P(('dp', 'mask')), parts along dimension 0
- visible_index: int32 [32, 51], P('dp'), parts along dimension 0, may hold values from 0 to 255, as said below
- embed_w: bfloat16 [768, 1024], replicated
- w_qkv: bfloat16 [1024, 3072], replicated, may hold values from -0.1875 to 0.1875
- w_out: bfloat16 [1024, 1024], replicated, may hold values from -0.1875 to 0.1875
- mask_embed: bfloat16 [1024], replicated, may hold values from -4 to 4
- dec_in: bfloat16 [1024, 768], replicated, may hold values from -0.1875 to 0.1875
- conv_w: bfloat16 [3, 16, 48, 48], replicated, may hold values from -0.5 to 0.5
- dec_out: bfloat16 [768, 1024], replicated, may hold values from -0.21875 to 0.21875
Outputs:
- embed_grad: float32 [6144, 1024], P(('dp', 'mask')), parts along dimension 0
- copy_loss: float32 [32], P(('dp', 'mask')), parts along dimension 0
There are 8 independent parts, one for each index of `dp`. A program takes and returns all parts, laid end to end along the dimension named above; an argument that names none is the same for every part. Nothing has to cross between parts.
Inputs may be any that keep to these rules, and one draw needn't show every extreme that they name: `visible_index`: each row lists 51 different patches; among the 64 patches of one index of mask (patches k * 64 to (k + 1) * 64 - 1) a row lists at most 26, and in every row some index's patches reach 26.
All inputs are finite; a program needn't handle non-finite values.
Results may differ from a plain program's by a relative error of at most 0.02.
Values may be sent and summed in bfloat16 or wider, within the bound.
No kernel may reach another device: no remote copies, remote signals or barrier semaphores. Data moves between devices by JAX's collectives and lax.ppermute only.
A program may use at most 128 MiB of HBM per device.

v0:
```python
import math
import jax
import jax.numpy as jnp
from jax import lax
from jax.sharding import PartitionSpec as P

D = 1024
HEADS = 16
DD = 768
GROUPS = 16
EPSILON = 1e-06


def row_norm(values):
    average = jnp.mean(values, axis=-1, keepdims=True)
    centred = values - average
    spread = jnp.mean(centred * centred, axis=-1, keepdims=True)
    return centred * lax.rsqrt(spread + EPSILON)


def head_norm(values):
    return values * lax.rsqrt(jnp.mean(values * values, axis=-1, keepdims=True) + EPSILON)


def mix_heads(queries, key_rows, values):
    score_scale = 1.0 / math.sqrt(queries.shape[-1])
    scores = (
        jnp.einsum("qhd,khd->hqk", queries, key_rows, preferred_element_type=jnp.float32)
        * score_scale
    )
    exponent = jnp.exp(scores)
    weights = (exponent / jnp.sum(exponent, axis=-1, keepdims=True)).astype(jnp.bfloat16)
    mixed = jnp.einsum("hqk,khd->qhd", weights, values, preferred_element_type=jnp.float32)
    return mixed.astype(jnp.bfloat16)


def split_project(projected):
    queries = head_norm(projected[:, 0].astype(jnp.float32)).astype(jnp.bfloat16)
    key_rows = head_norm(projected[:, 1].astype(jnp.float32)).astype(jnp.bfloat16)
    return mix_heads(queries, key_rows, projected[:, 2])


def attention_branch(inputs, w_qkv, w_out):
    row_count = inputs.shape[0]
    normed = row_norm(inputs.astype(jnp.float32)).astype(jnp.bfloat16)
    projected = jnp.dot(normed, w_qkv, preferred_element_type=jnp.float32).astype(jnp.bfloat16)
    context = split_project(projected.reshape(row_count, 3, HEADS, D // HEADS))
    return jnp.dot(context.reshape(row_count, D), w_out, preferred_element_type=jnp.float32)


def decoder_output(visible_out, positions, total_rows, mask_embed, dec_in, conv_w, dec_out):
    canvas = jnp.broadcast_to(mask_embed, (total_rows, D)).at[positions].set(visible_out)
    lowered = jnp.dot(canvas, dec_in, preferred_element_type=jnp.float32).astype(jnp.bfloat16)
    grouped = lowered.reshape(total_rows, GROUPS, DD // GROUPS)
    padded = jnp.pad(grouped, ((1, 1), (0, 0), (0, 0)))
    convolved = jnp.zeros((total_rows, GROUPS, DD // GROUPS), jnp.float32)
    for offset in range(3):
        convolved = convolved + jnp.einsum(
            "pgi,gio->pgo",
            padded[offset : offset + total_rows],
            conv_w[offset],
            preferred_element_type=jnp.float32,
        )
    activated = jax.nn.gelu(row_norm(convolved.reshape(total_rows, DD)), approximate=False)
    hidden = (lowered.astype(jnp.float32) + activated).astype(jnp.bfloat16)
    return jnp.dot(hidden, dec_out, preferred_element_type=jnp.float32)


def copy_terms(visible_in, positions, targets, w_qkv, w_out, mask_embed, dec_in, conv_w, dec_out):
    total_rows = targets.shape[0]
    visible_out = (
        visible_in.astype(jnp.float32) + attention_branch(visible_in, w_qkv, w_out)
    ).astype(jnp.bfloat16)
    predicted = decoder_output(
        visible_out, positions, total_rows, mask_embed, dec_in, conv_w, dec_out
    )
    slot_ids = jnp.arange(total_rows, dtype=jnp.int32)
    seen = jnp.max((slot_ids[:, None] == positions[None, :]).astype(jnp.float32), axis=1)
    mismatch = (predicted - targets.astype(jnp.float32)) * (1.0 - seen)[:, None]
    return jnp.sum(mismatch * mismatch)


def on_device(patches, visible_index, embed_w, w_qkv, w_out, mask_embed, dec_in, conv_w, dec_out):
    tok_rows = patches.shape[0]
    group_size = lax.axis_size("mask")
    own_index = lax.axis_index("mask")
    head_dim = D // HEADS
    heads_here = HEADS // group_size
    head_width = heads_here * head_dim
    copies = visible_index.shape[0]
    visible_count = visible_index.shape[1]
    total_rows = tok_rows * group_size
    positions = lax.dynamic_index_in_dim(visible_index, own_index, 0, keepdims=False)
    own_embedded = jnp.dot(patches, embed_w, preferred_element_type=jnp.float32).astype(
        jnp.bfloat16
    )
    embedded, clip_pixels = (
        lax.all_gather(own_embedded, "mask", axis=0, tiled=True),
        lax.all_gather(patches, "mask", axis=0, tiled=True),
    )
    visible_in = embedded[positions]
    normed = row_norm(embedded.astype(jnp.float32)).astype(jnp.bfloat16)
    own_cols = lax.dynamic_slice_in_dim(
        w_qkv.reshape(D, 3, D), own_index * head_width, head_width, 2
    )
    projected = jnp.einsum(
        "sd,dtw->stw", normed, own_cols, preferred_element_type=jnp.float32
    ).astype(jnp.bfloat16)
    context = split_project(projected.reshape(total_rows, 3, heads_here, head_dim))
    out_rows = lax.dynamic_slice_in_dim(w_out, own_index * head_width, head_width, 0)
    partial_value = jnp.dot(
        context.reshape(total_rows, head_width), out_rows, preferred_element_type=jnp.float32
    )
    branch = lax.psum(partial_value.astype(jnp.bfloat16), "mask").astype(jnp.float32)
    all_targets = row_norm(branch).astype(jnp.bfloat16)

    def objective(rows_in):
        return copy_terms(
            rows_in, positions, all_targets, w_qkv, w_out, mask_embed, dec_in, conv_w, dec_out
        )

    squares, pullback = jax.vjp(objective, visible_in)
    factor = 0.5 / math.sqrt(copies * visible_count)
    (grad_in,) = pullback(jnp.ones_like(squares) * factor)
    copy_loss = jnp.reshape(squares / ((total_rows - visible_count) * D), (1,))
    own_cols = lax.all_to_all(patches, "mask", split_axis=1, concat_axis=0, tiled=True)
    flat_index = visible_index.reshape(copies * visible_count)
    gathered = own_cols[flat_index]
    embed_grad = jnp.einsum(
        "vc,vd->cd",
        gathered,
        lax.all_gather(grad_in, "mask", axis=0, tiled=True),
        preferred_element_type=jnp.float32,
    )
    return (embed_grad, copy_loss)


def solution(mesh):
    placed = (P(("dp", "mask"), None), P("dp", None), P(), P(), P(), P(), P(), P(), P())
    return jax.shard_map(
        on_device,
        mesh=mesh,
        in_specs=placed,
        out_specs=(P(("dp", "mask"), None), P(("dp", "mask"))),
        check_vma=False,
    )
```

profile of v0, /device:TPU:0, one launch (start us, length us, event | category | flops | bytes accessed | tf_op | source)
XLA Modules:
  0.0 134.3 jit_solution(9758933965294009839)
XLA Ops:
  7.2 2.0 %convolution_convert_fusion.14 = bf16[64,1024]{1,0:T(8,128)(2,1)S(1)} fusion(bf16[64,768]{1,0:T(8,128)(2,1)} %param.9, bf16[768,1024]{1,0:T(8,128)(2,1)} %param.11), kind=kOutput, calls=%fused_computation.52 | convolution fusion | flops 100728832 | bytes 1802240 | tf_op jit(solution)/shard_map/dot_general | solution.py:94
  9.2 11.5 %all_gather.6 = bf16[256,1024]{1,0:T(8,128)(2,1)S(1)} all-gather(bf16[64,1024]{1,0:T(8,128)(2,1)S(1)} %convolution_convert_fusion.14), channel_id=1, replica_groups=mesh['dp'=8,'mask'=4] {'mask'}, dimensions={0}, use_global_device_ids=true | all-gather | bytes 655360 | tf_op jit(solution)/shard_map/all_gather | solution.py:98
  21.2 8.7 %copy.84 = bf16[1024,3072]{0,1:T(8,128)(2,1)} copy(bf16[1024,3072]{1,0:T(8,128)(2,1)} %param.12) | data formatting | bytes 12582912 | tf_op args[3]
  29.9 2.1 %fusion.4 = bf16[256,3,256]{0,2,1:T(8,128)(2,1)S(1)} fusion(bf16[1024,3,1024]{0,2,1:T(8,128)(2,1)} %bitcast.173, s32[]{:T(128)S(6)} %select_n.51, bf16[256,1024]{1,0:T(8,128)(2,1)S(1)} %all_gather.6, f32[256]{0:T(256)S(1)} %add_rsqrt_fusion.3, f32[256]{0:T(256)S(1)} %broadcast_multiply_fusion.2), kind=kOutput, calls=%fused_computation.21 | convolution fusion | flops 403898368 | bytes 2492420 | tf_op jit(solution)/shard_map/sd,dtw->stw/dot_general | solution.py:106
  32.1 1.3 %fusion.2 = f32[4,256,256]{1,2,0:T(8,128)} fusion(f32[256,4]{0,1:T(4,128)S(1)} %get-tuple-element.31, f32[256,4]{0,1:T(4,128)S(1)} %get-tuple-element.32, bf16[256,3,4,64]{0,3,2,1:T(8,128)(2,1)S(1)} %bitcast.182), kind=kOutput, calls=%fused_computation.10 | convolution fusion | flops 34209792 | bytes 1318912 | tf_op jit(solution)/shard_map/qhd,khd->hqk/dot_general | solution.py:28
  33.4 1.8 %convolution_convert_fusion.13 = bf16[4,64,256]{2,1,0:T(8,128)(2,1)S(1)} fusion(f32[4,256,256]{1,2,0:T(8,128)} %fusion.2, bf16[256,3,4,64]{0,3,2,1:T(8,128)(2,1)S(1)} %bitcast.183), kind=kOutput, calls=%fused_computation.51 | convolution fusion | flops 34145536 | bytes 2359296 | tf_op jit(solution)/shard_map/hqk,khd->qhd/dot_general | solution.py:33
  35.3 1.1 convolution_convert_fusion.1
  36.6 0.7 copy.73
  37.3 3.3 %all-to-all-start = ((bf16[64,4,192]{2,0,1:T(8,128)(2,1)}), bf16[64,4,192]{2,0,1:T(8,128)(2,1)S(1)}, u32[]{:S(2)}, u32[]{:S(2)}) async-start(bf16[64,4,192]{2,0,1:T(8,128)(2,1)} %copy.73), calls=%async_computation | async-start | bytes 262144 | tf_op jit(solution)/shard_map/all_to_all | solution.py:126
  40.7 0.6 compare_and_fusion
  41.3 0.6 reshape.257
  41.9 0.7 gather_fusion.2
  43.2 4.0 %convolution_convert_fusion = bf16[51,3072]{1,0:T(8,128)(2,1)S(1)} fusion(bf16[1024,3072]{1,0:T(8,128)(2,1)} %param.12, bf16[51,1024]{1,0:T(8,128)(2,1)S(1)} %gather_fusion.2, f32[51]{0:T(128)S(1)} %fusion.116, f32[51]{0:T(128)S(1)} %broadcast_multiply_fusion.4), kind=kOutput, calls=%fused_computation.6 | convolution fusion | flops 321229824 | bytes 6709656 | tf_op jit(solution)/shard_map/jvp()/dot_general | solution.py:46
  48.7 0.6 copy-done.26
  49.9 1.1 scatter_custom_fusion
  51.0 1.3 gather_fusion.1
  52.3 1.0 broadcast_compare_fusion
  53.4 0.9 compare_select_fusion
  54.8 0.6 copy-done.1
  55.4 1.5 %scatter_fusion = bf16[256,1024]{1,0:T(8,128)(2,1)S(1)} fusion(bf16[256,1024]{1,0:T(8,128)(2,1)S(1)} %copy-done.1, s32[51]{0:T(128)S(1)} %fusion.115, bf16[51,1024]{1,0:T(8,128)(2,1)S(1)} %fusion.24), kind=kCustom, calls=%fused_computation.5 | custom fusion | flops 52224 | bytes 313548 | tf_op jit(solution)/shard_map/jvp()/scatter-add | solution.py:52
  56.9 2.7 %convolution_convert_fusion.7 = bf16[256,768]{1,0:T(8,128)(2,1)} fusion(bf16[256,1024]{1,0:T(8,128)(2,1)S(1)} %scatter_fusion, bf16[1024,768]{1,0:T(8,128)(2,1)} %param.15), kind=kOutput, calls=%fused_computation.26 | convolution fusion | flops 402849792 | bytes 2490368 | tf_op jit(solution)/shard_map/jvp()/dot_general | solution.py:53
  59.6 1.2 copy.79
  60.8 1.3 fusion.62
  62.1 1.2 convolution_add_fusion.1
  63.4 1.4 %fusion.128 = (f32[256]{0:T(256)S(1)}, f32[16,256,48]{1,2,0:T(8,128)S(1)}) fusion(f32[16,256,48]{1,2,0:T(8,128)S(1)} %convolution_add_fusion.1, bf16[256,16,48]{0,2,1:T(8,128)(2,1)S(1)} %bitcast.179, bf16[3,16,48,48]{3,2,1,0:T(8,128)(2,1)} %param.16), kind=kOutput, calls=%fused_computation.234 | convolution fusion | flops 19267328 | bytes 2163712 | tf_op jit(solution)/shard_map/jvp(pgi,gio->pgo)/dot_general | solution.py:58
  64.9 0.6 fusion.114
  65.5 1.1 copy.83
  66.7 0.8 convert_reduce_fusion.3
  67.5 0.6 broadcast_multiply_fusion
  68.1 0.6 compare_select_fusion.1
  68.7 1.3 multiply_divide_fusion
  70.0 0.6 pad_clamp_fusion.1
  70.6 1.8 %gather_fusion = bf16[204,192]{1,0:T(8,128)(2,1)} fusion(bf16[256,192]{1,0:T(8,128)(2,1)S(1)} %bitcast.171, s32[1024]{0:T(1024)} %pad_clamp_fusion.1), kind=kCustom, calls=%fused_computation | custom fusion | bytes 157488 | tf_op jit(solution)/shard_map/gather | solution.py:128
  72.4 10.7 %all-reduce.9.cloned.1.call-done = bf16[256,1024]{1,0:T(8,128)(2,1)} async-done(((bf16[256,1024]{1,0:T(8,128)(2,1)}), bf16[256,1024]{1,0:T(8,128)(2,1)}) %all-reduce.9.cloned.1.call-update) | async-done | bytes 524304 | tf_op jit(solution)/shard_map/psum | solution.py:114
  83.1 1.2 convert_reduce_fusion
  84.3 1.3 fusion.25
  85.7 4.8 %multiply_reduce_fusion = (f32[]{:T(128)}, f32[256,1024]{1,0:T(8,128)S(1)}) fusion(f32[256]{0:T(256)} %get-tuple-element.12, f32[256]{0:T(256)S(1)} %add_rsqrt_fusion.2, f32[256]{0:T(256)S(1)} %broadcast_multiply_fusion.1, bf16[256,1024]{1,0:T(8,128)(2,1)} %all-reduce.9.cloned.1.call-done, bf16[768,1024]{1,0:T(8,128)(2,1)} %param.17, ...), kind=kOutput, calls=%fused_computation.64 | convolution fusion | flops 418971648 | bytes 4330500 | tf_op jit(solution)/shard_map/jvp()/dot_general | solution.py:66
  90.5 3.5 %multiply_reduce_fusion.1 = (f32[256]{0:T(256)S(1)}, bf16[256,768]{1,0:T(8,128)(2,1)S(1)}) fusion(f32[256,768]{1,0:T(8,128)S(1)} %copy-done.2, f32[256]{0:T(256)S(1)} %copy-done.23, f32[256]{0:T(256)S(1)} %copy-done.34, bf16[768,1024]{1,0:T(8,128)(2,1)S(1)} %copy-done.40, f32[256,1024]{1,0:T(8,128)S(1)} %get-tuple-element.28, f32[256]{0:T(256)S(1)} %copy-done.37), kind=kOutput, calls=%fused_computation.87 | convolution fusion | flops 419495680 | bytes 3805184 | tf_op jit(solution)/shard_map/transpose(jvp())/dot_general | solution.py:66
  94.1 2.5 %fusion.125 = (f32[256]{0:T(256)S(1)}, f32[256,768]{1,0:T(8,128)S(1)}) fusion(f32[256]{0:T(256)S(1)} %multiply_multiply_fusion.8, bf16[256,768]{1,0:T(8,128)(2,1)S(1)} %get-tuple-element.18, f32[256]{0:T(256)S(1)} %copy-done.34, f32[256,768]{1,0:T(8,128)S(1)} %copy-done.2, f32[256]{0:T(256)S(1)} %copy-done.23), kind=kLoop, calls=%fused_computation.231 | loop fusion | flops 15531776 | bytes 1970176 | tf_op jit(solution)/shard_map/transpose(jvp())/reduce_sum | solution.py:16
  96.7 0.8 broadcast_add_fusion
  97.5 1.2 copy.86
  100.4 2.0 %convolution_convert_fusion.2 = bf16[256,1024]{1,0:T(8,128)(2,1)S(1)} fusion(bf16[1024,768]{1,0:T(8,128)(2,1)} %param.15, bf16[256,768]{1,0:T(8,128)(2,1)S(1)} %copy-done.10, bf16[256,768]{1,0:T(8,128)(2,1)S(1)} %copy.90), kind=kOutput, calls=%fused_computation.20 | convolution fusion | flops 403111936 | bytes 2883584 | tf_op jit(solution)/shard_map/transpose(jvp())/dot_general | solution.py:53
  102.4 0.8 gather_fusion.3
  103.3 1.6 %convolution_convert_fusion.16 = bf16[51,1024]{1,0:T(8,128)(2,1)S(1)} fusion(bf16[1024,1024]{1,0:T(8,128)(2,1)S(1)} %copy-done, pred[51,1024]{1,0:T(8,128)(4,1)} %copy-done.13, bf16[51,1024]{1,0:T(8,128)(2,1)S(1)} %gather_fusion.3, pred[51]{0:T(512)(128)(4,1)} %get-tuple-element.4), kind=kOutput, calls=%fused_computation.56 | convolution fusion | flops 107111424 | bytes 2358323 | tf_op jit(solution)/shard_map/transpose(jvp())/dot_general | solution.py:48
  106.6 0.6 fusion.58
  108.7 5.0 %fusion.77 = (f32[51]{0:T(128)S(1)}, f32[51,1024]{1,0:T(8,128)S(1)}) fusion(bf16[51,1024]{1,0:T(8,128)(2,1)S(1)} %gather_fusion.2, f32[51]{0:T(128)S(1)} %copy-done.21, bf16[51,3072]{1,0:T(8,128)(2,1)S(1)} %reshape.268, bf16[1024,3072]{1,0:T(8,128)(2,1)} %param.12), kind=kOutput, calls=%fused_computation.151 | convolution fusion | flops 321177536 | bytes 6918552 | tf_op jit(solution)/shard_map/transpose(jvp())/dot_general | solution.py:46
  114.2 10.2 %all-gather = bf16[4,51,1024]{2,1,0:T(8,128)(2,1)S(1)} all-gather(bf16[1,51,1024]{2,1,0:T(8,128)(2,1)S(1)} %fusion.105), channel_id=1, replica_groups=mesh['dp'=8,'mask'=4] {'mask'}, dimensions={0}, use_global_device_ids=true | all-gather | bytes 522240 | tf_op jit(solution)/shard_map/all_gather | solution.py:132
  124.5 1.2 fusion.129
  (135 shorter events, 9.4 us)
Async XLA Ops:
  7.2 28.1 %copy-start = (bf16[1024,1024]{1,0:T(8,128)(2,1)S(1)}, bf16[1024,1024]{1,0:T(8,128)(2,1)}, u32[]{:S(2)}) copy-start(bf16[1024,1024]{1,0:T(8,128)(2,1)} %param.13) | copy-start | bytes 6291460
  7.2 75.9 %all-reduce.9.cloned.1.call-start = ((), (), s32[]{:S(2)}) async-start(), calls=%async_computation.1 | async-start | bytes 1048576 | tf_op jit(solution)/shard_map/psum | solution.py:114
  35.3 1.2 copy-start.17
  35.3 5.4 %copy-start.35 = (s32[4,51]{1,0:T(4,128)S(1)}, s32[4,51]{1,0:T(4,128)}, u32[]{:S(2)}) copy-start(s32[4,51]{1,0:T(4,128)} %param.10) | copy-start | bytes 2452
  37.3 33.3 %all-to-all-start = ((bf16[64,4,192]{2,0,1:T(8,128)(2,1)}), bf16[64,4,192]{2,0,1:T(8,128)(2,1)S(1)}, u32[]{:S(2)}, u32[]{:S(2)}) async-start(bf16[64,4,192]{2,0,1:T(8,128)(2,1)} %copy.73), calls=%async_computation | async-start | bytes 262144 | tf_op jit(solution)/shard_map/all_to_all | solution.py:126
  40.6 11.7 %copy-start.29 = (u32[51]{0:T(128)}, u32[51]{0:T(128)S(1)}, u32[]{:S(2)}) copy-start(u32[51]{0:T(128)S(1)} %iota_add_fusion) | copy-start | bytes 616
  41.9 9.1 %copy-start.28 = (s32[1024]{0:T(1024)}, s32[1024]{0:T(1024)S(1)}, u32[]{:S(2)}) copy-start(s32[1024]{0:T(1024)S(1)} %pad_clamp_fusion) | copy-start | bytes 12292
  42.7 0.5 copy-start.20
  42.9 4.3 %copy-start.38 = (f32[51]{0:T(128)}, f32[51]{0:T(128)S(1)}, u32[]{:S(2)}) copy-start(f32[51]{0:T(128)S(1)} %fusion.75) | copy-start | bytes 616
  43.2 4.0 %copy-start.31 = (f32[51]{0:T(128)}, f32[51]{0:T(128)S(1)}, u32[]{:S(2)}) copy-start(f32[51]{0:T(128)S(1)} %fusion.116) | copy-start | bytes 616
  47.8 1.9 %copy-start.5 = (bf16[51,1,16,64]{3,2,1,0:T(8,128)(2,1)}, bf16[51,1,16,64]{3,2,1,0:T(8,128)(2,1)S(1)}, u32[]{:S(2)}) copy-start(bf16[51,1,16,64]{3,2,1,0:T(8,128)(2,1)S(1)} %get-tuple-element.9) | copy-start | bytes 313348
  47.8 1.9 %copy-start.7 = (bf16[51,1,16,64]{3,2,1,0:T(8,128)(2,1)}, bf16[51,1,16,64]{3,2,1,0:T(8,128)(2,1)S(1)}, u32[]{:S(2)}) copy-start(bf16[51,1,16,64]{3,2,1,0:T(8,128)(2,1)S(1)} %get-tuple-element.10) | copy-start | bytes 313348
  47.8 1.9 %copy-start.11 = (bf16[51,1,16,64]{3,2,1,0:T(8,128)(2,1)}, bf16[51,1,16,64]{3,2,1,0:T(8,128)(2,1)S(1)}, u32[]{:S(2)}) copy-start(bf16[51,1,16,64]{3,2,1,0:T(8,128)(2,1)S(1)} %get-tuple-element.8) | copy-start | bytes 313348
  48.7 0.6 copy-start.26
  48.7 0.9 copy-start.14
  49.9 3.5 %copy-start.36 = (bf16[1024]{0:T(1024)(128)(2,1)S(1)}, bf16[1024]{0:T(1024)(128)(2,1)}, u32[]{:S(2)}) copy-start(bf16[1024]{0:T(1024)(128)(2,1)} %param.14) | copy-start | bytes 6148
  53.4 0.9 copy-start.13
  54.3 1.0 copy-start.1
  64.7 0.8 copy-start.22
  64.9 0.6 copy-start.24
  65.5 20.1 %copy-start.18 = (bf16[256,768]{1,0:T(8,128)(2,1)S(1)}, bf16[256,768]{1,0:T(8,128)(2,1)}, u32[]{:S(2)}) copy-start(bf16[256,768]{1,0:T(8,128)(2,1)} %convolution_convert_fusion.7) | copy-start | bytes 1179652
  66.7 19.0 %copy-start.2 = (f32[256,768]{1,0:T(8,128)S(1)}, f32[256,768]{1,0:T(8,128)}, u32[]{:S(2)}) copy-start(f32[256,768]{1,0:T(8,128)} %copy.83) | copy-start | bytes 2359300
  85.6 4.9 %copy-start.23 = (f32[256]{0:T(256)S(1)}, f32[256]{0:T(256)}, u32[]{:S(2)}) copy-start(f32[256]{0:T(256)} %copy-done.22) | copy-start | bytes 3076
  85.6 4.8 %copy-start.34 = (f32[256]{0:T(256)S(1)}, f32[256]{0:T(256)}, u32[]{:S(2)}) copy-start(f32[256]{0:T(256)} %fusion.114) | copy-start | bytes 3076
  85.7 4.8 %copy-start.37 = (f32[256]{0:T(256)S(1)}, f32[256]{0:T(256)}, u32[]{:S(2)}) copy-start(f32[256]{0:T(256)} %get-tuple-element.11) | copy-start | bytes 3076
  85.7 4.8 %copy-start.40 = (bf16[768,1024]{1,0:T(8,128)(2,1)S(1)}, bf16[768,1024]{1,0:T(8,128)(2,1)}, u32[]{:S(2)}) copy-start(bf16[768,1024]{1,0:T(8,128)(2,1)} %param.17) | copy-start | bytes 4718596
  90.5 3.6 %copy-start.25 = (f32[256]{0:T(256)S(1)}, f32[256]{0:T(256)}, u32[]{:S(2)}) copy-start(f32[256]{0:T(256)} %copy-done.24) | copy-start | bytes 3076
  94.0 2.6 %copy-start.9 = (bf16[256,768]{1,0:T(8,128)(2,1)}, bf16[256,768]{1,0:T(8,128)(2,1)S(1)}, u32[]{:S(2)}) copy-start(bf16[256,768]{1,0:T(8,128)(2,1)S(1)} %get-tuple-element.18) | copy-start | bytes 1179652
  96.6 2.1 %copy-start.3 = (bf16[3,16,48,48]{3,2,1,0:T(8,128)(2,1)S(1)}, bf16[3,16,48,48]{3,2,1,0:T(8,128)(2,1)}, u32[]{:S(2)}) copy-start(bf16[3,16,48,48]{3,2,1,0:T(8,128)(2,1)} %param.16) | copy-start | bytes 663556
  99.4 1.0 copy-start.10
  103.2 1.9 %copy-start.15 = (f32[16,51,51]{1,2,0:T(8,128)S(1)}, f32[16,51,51]{1,2,0:T(8,128)}, u32[]{:S(2)}) copy-start(f32[16,51,51]{1,2,0:T(8,128)} %copy-done.14) | copy-start | bytes 499396
  103.2 1.9 %copy-start.27 = (f32[16,51]{1,0:T(8,128)S(1)}, f32[16,51]{1,0:T(8,128)}, u32[]{:S(2)}) copy-start(f32[16,51]{1,0:T(8,128)} %copy-done.26) | copy-start | bytes 9796
  104.9 0.9 copy-start.12
  104.9 0.9 copy-start.19
  105.1 1.0 copy-start.6
  105.1 1.0 copy-start.8
  107.8 0.8 copy-start.21
  108.6 5.1 %copy-start.39 = (f32[51]{0:T(128)S(1)}, f32[51]{0:T(128)}, u32[]{:S(2)}) copy-start(f32[51]{0:T(128)} %copy-done.38) | copy-start | bytes 616
  108.6 5.1 %copy-start.32 = (f32[51]{0:T(128)S(1)}, f32[51]{0:T(128)}, u32[]{:S(2)}) copy-start(f32[51]{0:T(128)} %copy-done.31) | copy-start | bytes 616
  108.7 5.3 %copy-start.4 = (u32[51,1024]{1,0:T(8,128)S(1)}, u32[51,1024]{1,0:T(8,128)}, u32[]{:S(2)}) copy-start(u32[51,1024]{1,0:T(8,128)} %gather_fusion.1) | copy-start | bytes 626692
  108.7 5.3 %copy-start.30 = (u32[51]{0:T(128)S(1)}, u32[51]{0:T(128)}, u32[]{:S(2)}) copy-start(u32[51]{0:T(128)} %copy-done.29) | copy-start | bytes 616
  108.7 5.3 %copy-start.33 = (pred[51]{0:T(512)(128)(4,1)S(1)}, pred[51]{0:T(512)(128)(4,1)}, u32[]{:S(2)}) copy-start(pred[51]{0:T(512)(128)(4,1)} %get-tuple-element.4) | copy-start | bytes 157
  113.7 10.8 %copy-start.16 = (bf16[204,192]{1,0:T(8,128)(2,1)S(1)}, bf16[204,192]{1,0:T(8,128)(2,1)}, u32[]{:S(2)}) copy-start(bf16[204,192]{1,0:T(8,128)(2,1)} %gather_fusion) | copy-start | bytes 235012
Sparse Core Ops, SparseCore 0:
  36.6 46.4 all-reduce.8
where the time goes:
time: 135 us; the launch traced here: 134 us
  matrix products  40.8 us (30%)
  local copies, waits for them, and re-layouts  23.6 us (17%)
  blocking collectives  21.7 us (16%)
  other arithmetic  17.5 us (13%)
  between operations  16.7 us (12%)
  waiting for transfers between devices  10.7 us (8%)
  starting transfers between devices  3.36 us (2%)
    all_gather x1, blocking collectives, on_device(): lax.all_gather(own_embedded, 'mask', axis=0, tiled=True)  11.5 us
    unnamed x84, local copies, waits for them, and re-layouts  11.3 us
    psum x1, waiting for transfers between devices, on_device(): lax.psum(partial_value.astype(jnp.bfloat16), 'mask').astype(jnp.float32)  10.7 us
    all_gather x1, blocking collectives, on_device(): lax.all_gather(grad_in, 'mask', axis=0, tiled=True)  10.2 us
    dot_general x2, matrix products, attention_branch(): jnp.dot(normed, w_qkv, preferred_element_type=jnp.float32)  9 us
    dot_general x2, matrix products, decoder_output(): return jnp.dot(hidden, dec_out, preferred_element_type=jnp.float32)  8.34 us
    dot_general x2, matrix products, decoder_output(): jnp.dot(canvas, dec_in, preferred_element_type=jnp.float32)  4.74 us
    dot_general x6, matrix products, decoder_output(): jnp.einsum('pgi,gio->pgo', padded[offset:offset + total_rows], conv_w[off...  4.62 us
  transfers between devices with their start and end apart: 2, of which 1 were waited for; matrix products, arithmetic and copies ran while one was open for 23% of the time, Pallas kernels for 0%

commit v1 on v0

--- a/solution.py
+++ b/solution.py
@@ -111,7 +111,9 @@
     partial_value = jnp.dot(
         context.reshape(total_rows, head_width), out_rows, preferred_element_type=jnp.float32
     )
-    branch = lax.psum(partial_value.astype(jnp.bfloat16), "mask").astype(jnp.float32)
+    branch = jnp.sum(
+        lax.all_gather(partial_value.astype(jnp.bfloat16), axis_name="mask"), axis=0
+    ).astype(jnp.float32)
     all_targets = row_norm(branch).astype(jnp.bfloat16)
 
     def objective(rows_in):

time: 135 us -> 125 us (0.926)
  waiting for transfers between devices: 10.7 us -> 0.02 us
  matrix products: 40.8 us -> 42.9 us
  other arithmetic: 17.5 us -> 16.1 us
    psum x1 -> x0, waiting for transfers between devices: 10.7 us -> none  [on_device(): lax.psum(partial_value.astype(jnp.bfloat16), 'mask').astype(jnp.float32)]
    reduce_sum x0 -> x1, other arithmetic: none -> 2.02 us  [on_device(): jnp.sum(lax.all_gather(partial_value.astype(jnp.bfloat16), axis_name='mas...]
    dot_general x6, matrix products: 4.62 us -> 6.14 us  [decoder_output(): jnp.einsum('pgi,gio->pgo', padded[offset:offset + total_rows], conv_w[off...]
    unnamed x84 -> x86, local copies, waits for them, and re-layouts: 11.3 us -> 10.7 us
  transfers between devices with their start and end apart: 2 -> 2, of which waited for: 1 -> 0; matrix products, arithmetic and copies ran while one was open for 23% -> 24% of each run, Pallas kernels for 0% -> 0%
where the time goes in v1:
time: 125 us; the launch traced here: 124 us
  matrix products  42.9 us (34%)
  local copies, waits for them, and re-layouts  23 us (18%)
  blocking collectives  22.4 us (18%)
  between operations  16.6 us (13%)
  other arithmetic  16.1 us (13%)
  starting transfers between devices  3.36 us (3%)
    all_gather x1, blocking collectives, on_device(): lax.all_gather(own_embedded, 'mask', axis=0, tiled=True)  11.5 us
    all_gather x1, blocking collectives, on_device(): lax.all_gather(grad_in, 'mask', axis=0, tiled=True)  10.8 us
    unnamed x86, local copies, waits for them, and re-layouts  10.7 us
    dot_general x2, matrix products, attention_branch(): jnp.dot(normed, w_qkv, preferred_element_type=jnp.float32)  9.35 us
    dot_general x2, matrix products, decoder_output(): return jnp.dot(hidden, dec_out, preferred_element_type=jnp.float32)  8.2 us
    dot_general x6, matrix products, decoder_output(): jnp.einsum('pgi,gio->pgo', padded[offset:offset + total_rows], conv_w[off...  6.14 us
    dot_general x2, matrix products, decoder_output(): jnp.dot(canvas, dec_in, preferred_element_type=jnp.float32)  4.89 us
    dot_general x4, matrix products, mix_heads(): jnp.einsum('hqk,khd->qhd', weights, values, preferred_element_type=jnp.fl...  3.84 us
  transfers between devices with their start and end apart: 2, of which 0 were waited for; matrix products, arithmetic and copies ran while one was open for 24% of the time, Pallas kernels for 0%

profile of v1, /device:TPU:0, one launch (start us, length us, event | category | flops | bytes accessed | tf_op | source)
XLA Modules:
  0.0 124.4 jit_solution(12562598091952762614)
XLA Ops:
  7.2 2.0 %convolution_convert_fusion.14 = bf16[64,1024]{1,0:T(8,128)(2,1)S(1)} fusion(bf16[64,768]{1,0:T(8,128)(2,1)} %param.9, bf16[768,1024]{1,0:T(8,128)(2,1)} %param.11), kind=kOutput, calls=%fused_computation.52 | convolution fusion | flops 100728832 | bytes 1802240 | tf_op jit(solution)/shard_map/dot_general | solution.py:94
  9.2 11.5 %all_gather.12 = bf16[256,1024]{1,0:T(8,128)(2,1)S(1)} all-gather(bf16[64,1024]{1,0:T(8,128)(2,1)S(1)} %convolution_convert_fusion.14), channel_id=1, replica_groups=mesh['dp'=8,'mask'=4] {'mask'}, dimensions={0}, use_global_device_ids=true | all-gather | bytes 655360 | tf_op jit(solution)/shard_map/all_gather | solution.py:98
  21.2 8.7 %copy.84 = bf16[1024,3072]{0,1:T(8,128)(2,1)} copy(bf16[1024,3072]{1,0:T(8,128)(2,1)} %param.12) | data formatting | bytes 12582912 | tf_op args[3]
  29.9 2.1 %fusion.4 = bf16[256,3,256]{0,2,1:T(8,128)(2,1)S(1)} fusion(bf16[1024,3,1024]{0,2,1:T(8,128)(2,1)} %bitcast.174, s32[]{:T(128)S(6)} %select_n.51, bf16[256,1024]{1,0:T(8,128)(2,1)S(1)} %all_gather.12, f32[256]{0:T(256)S(1)} %add_rsqrt_fusion.3, f32[256]{0:T(256)S(1)} %broadcast_multiply_fusion.2), kind=kOutput, calls=%fused_computation.21 | convolution fusion | flops 403898368 | bytes 2492420 | tf_op jit(solution)/shard_map/sd,dtw->stw/dot_general | solution.py:106
  32.1 1.3 %fusion.2 = f32[4,256,256]{1,2,0:T(8,128)} fusion(f32[256,4]{0,1:T(4,128)S(1)} %get-tuple-element.31, f32[256,4]{0,1:T(4,128)S(1)} %get-tuple-element.32, bf16[256,3,4,64]{0,3,2,1:T(8,128)(2,1)S(1)} %bitcast.184), kind=kOutput, calls=%fused_computation.10 | convolution fusion | flops 34209792 | bytes 1318912 | tf_op jit(solution)/shard_map/qhd,khd->hqk/dot_general | solution.py:28
  33.4 1.9 %convolution_convert_fusion.13 = bf16[4,64,256]{2,1,0:T(8,128)(2,1)S(1)} fusion(f32[4,256,256]{1,2,0:T(8,128)} %fusion.2, bf16[256,3,4,64]{0,3,2,1:T(8,128)(2,1)S(1)} %bitcast.185), kind=kOutput, calls=%fused_computation.51 | convolution fusion | flops 34145536 | bytes 2359296 | tf_op jit(solution)/shard_map/hqk,khd->qhd/dot_general | solution.py:33
  35.3 1.1 convolution_convert_fusion.1
  36.6 0.7 copy.73
  37.3 3.3 %all-to-all-start = ((bf16[64,4,192]{2,0,1:T(8,128)(2,1)}), bf16[64,4,192]{2,0,1:T(8,128)(2,1)S(1)}, u32[]{:S(2)}, u32[]{:S(2)}) async-start(bf16[64,4,192]{2,0,1:T(8,128)(2,1)} %copy.73), calls=%async_computation | async-start | bytes 262144 | tf_op jit(solution)/shard_map/all_to_all | solution.py:128
  40.7 0.7 reshape.257
  41.3 0.7 gather_fusion.2
  42.7 4.4 %convolution_convert_fusion = bf16[51,3072]{1,0:T(8,128)(2,1)S(1)} fusion(bf16[1024,3072]{1,0:T(8,128)(2,1)} %param.12, bf16[51,1024]{1,0:T(8,128)(2,1)S(1)} %gather_fusion.2, f32[51]{0:T(128)S(1)} %fusion.116, f32[51]{0:T(128)S(1)} %broadcast_multiply_fusion.4), kind=kOutput, calls=%fused_computation.6 | convolution fusion | flops 321229824 | bytes 6709656 | tf_op jit(solution)/shard_map/jvp()/dot_general | solution.py:46
  48.3 0.5 fusion.127
  48.8 0.6 copy-done.25
  50.0 1.1 scatter_custom_fusion
  51.1 1.3 %gather_fusion.1 = u32[51,1024]{1,0:T(8,128)} fusion(u32[256,1024]{1,0:T(8,128)S(1)} %scatter_custom_fusion, s32[1024]{0:T(1024)S(1)} %pad_clamp_fusion), kind=kCustom, calls=%fused_computation.1 | custom fusion | bytes 417996 | tf_op jit(solution)/shard_map/jvp()/gather | solution.py:52
  52.4 0.9 compare_select_fusion
  53.4 1.1 broadcast_compare_fusion
  54.5 0.6 copy-done.12
  55.1 0.5 fusion.24
  55.6 1.5 %scatter_fusion = bf16[256,1024]{1,0:T(8,128)(2,1)S(1)} fusion(bf16[256,1024]{1,0:T(8,128)(2,1)S(1)} %copy-done.1, s32[51]{0:T(128)S(1)} %fusion.115, bf16[51,1024]{1,0:T(8,128)(2,1)S(1)} %fusion.24), kind=kCustom, calls=%fused_computation.5 | custom fusion | flops 52224 | bytes 313548 | tf_op jit(solution)/shard_map/jvp()/scatter-add | solution.py:52
  57.1 2.7 %convolution_convert_fusion.7 = bf16[256,768]{1,0:T(8,128)(2,1)} fusion(bf16[256,1024]{1,0:T(8,128)(2,1)S(1)} %scatter_fusion, bf16[1024,768]{1,0:T(8,128)(2,1)} %param.15), kind=kOutput, calls=%fused_computation.26 | convolution fusion | flops 402849792 | bytes 2490368 | tf_op jit(solution)/shard_map/jvp()/dot_general | solution.py:53
  59.9 1.2 copy.79
  61.0 1.3 %fusion.62 = f32[16,256,48]{1,2,0:T(8,128)S(1)} fusion(bf16[256,16,48]{0,2,1:T(8,128)(2,1)S(1)} %bitcast.178, bf16[3,16,48,48]{3,2,1,0:T(8,128)(2,1)} %param.16), kind=kOutput, calls=%fused_computation.126 | convolution fusion | flops 18874368 | bytes 1376256 | tf_op jit(solution)/shard_map/jvp(pgi,gio->pgo)/dot_general | solution.py:58
  62.4 1.2 convolution_add_fusion.1
  63.6 1.9 %fusion.128 = (f32[256]{0:T(256)}, f32[16,256,48]{1,2,0:T(8,128)S(1)}) fusion(f32[16,256,48]{1,2,0:T(8,128)S(1)} %convolution_add_fusion.1, bf16[256,16,48]{0,2,1:T(8,128)(2,1)S(1)} %bitcast.180, bf16[3,16,48,48]{3,2,1,0:T(8,128)(2,1)} %param.16), kind=kOutput, calls=%fused_computation.234 | convolution fusion | flops 19267328 | bytes 2163712 | tf_op jit(solution)/shard_map/jvp(pgi,gio->pgo)/dot_general | solution.py:58
  65.6 1.1 copy.83
  66.7 1.2 compare_and_fusion
  68.0 0.7 broadcast_multiply_fusion.3
  68.8 0.6 fusion.114
  69.4 0.6 broadcast_multiply_fusion
  70.0 0.6 multiply_divide_fusion
  70.6 1.7 %gather_fusion = bf16[204,192]{1,0:T(8,128)(2,1)} fusion(bf16[256,192]{1,0:T(8,128)(2,1)S(1)} %bitcast.172, s32[1024]{0:T(1024)S(1)} %pad_clamp_fusion.1), kind=kCustom, calls=%fused_computation | custom fusion | bytes 157488 | tf_op jit(solution)/shard_map/gather | solution.py:130
  72.3 2.0 %reduce_sum.250 = bf16[256,1024]{1,0:T(8,128)(2,1)S(1)} reduce(bf16[4,256,1024]{2,1,0:T(8,128)(2,1)} %bitcast.181, bf16[]{:T(256)} %constant.56.clone.1), dimensions={0}, to_apply=%region_14.15 | reduce | flops 786432 | bytes 2621442 | tf_op jit(solution)/shard_map/reduce_sum | solution.py:114
  74.8 4.7 %multiply_reduce_fusion = (f32[]{:T(128)}, f32[256,1024]{1,0:T(8,128)S(1)}) fusion(f32[256]{0:T(256)} %get-tuple-element.12, f32[256]{0:T(256)S(1)} %add_rsqrt_fusion.2, f32[256]{0:T(256)S(1)} %broadcast_multiply_fusion.1, bf16[256,1024]{1,0:T(8,128)(2,1)S(1)} %reduce_sum.250, bf16[768,1024]{1,0:T(8,128)(2,1)} %param.17, ...), kind=kOutput, calls=%fused_computation.64 | convolution fusion | flops 418971648 | bytes 4330500 | tf_op jit(solution)/shard_map/jvp()/dot_general | solution.py:66
  79.5 3.5 %multiply_reduce_fusion.1 = (f32[256]{0:T(256)S(1)}, bf16[256,768]{1,0:T(8,128)(2,1)S(1)}) fusion(f32[256,768]{1,0:T(8,128)S(1)} %copy-done.2, f32[256]{0:T(256)S(1)} %copy-done.22, f32[256]{0:T(256)S(1)} %copy-done.34, bf16[768,1024]{1,0:T(8,128)(2,1)S(1)} %copy-done.41, f32[256,1024]{1,0:T(8,128)S(1)} %get-tuple-element.28, f32[256]{0:T(256)S(1)} %copy-done.38), kind=kOutput, calls=%fused_computation.87 | convolution fusion | flops 419495680 | bytes 3805184 | tf_op jit(solution)/shard_map/transpose(jvp())/dot_general | solution.py:66
  83.1 2.5 %fusion.125 = (f32[256]{0:T(256)S(1)}, f32[256,768]{1,0:T(8,128)S(1)}) fusion(f32[256]{0:T(256)S(1)} %multiply_multiply_fusion.8, bf16[256,768]{1,0:T(8,128)(2,1)S(1)} %get-tuple-element.18, f32[256]{0:T(256)S(1)} %copy-done.34, f32[256,768]{1,0:T(8,128)S(1)} %copy-done.2, f32[256]{0:T(256)S(1)} %copy-done.22), kind=kLoop, calls=%fused_computation.231 | loop fusion | flops 15531776 | bytes 1970176 | tf_op jit(solution)/shard_map/transpose(jvp())/reduce_sum | solution.py:16
  85.7 0.8 broadcast_add_fusion
  86.5 1.2 copy.86
  87.7 1.2 fusion.12
  89.9 2.2 %convolution_convert_fusion.2 = bf16[256,1024]{1,0:T(8,128)(2,1)S(1)} fusion(bf16[1024,768]{1,0:T(8,128)(2,1)} %param.15, bf16[256,768]{1,0:T(8,128)(2,1)} %copy-done.9, bf16[256,768]{1,0:T(8,128)(2,1)S(1)} %copy.90), kind=kOutput, calls=%fused_computation.20 | convolution fusion | flops 403111936 | bytes 2883584 | tf_op jit(solution)/shard_map/transpose(jvp())/dot_general | solution.py:53
  92.1 0.9 gather_fusion.3
  93.0 0.8 convolution_convert_fusion.16
  94.0 1.3 %fusion.21 = bf16[51,1,16,64]{3,0,2,1:T(8,128)(2,1)S(1)} fusion(bf16[51,16,64]{2,1,0:T(8,128)(2,1)S(1)} %reshape.267, f32[16,51,51]{1,2,0:T(8,128)} %copy-done.14, f32[16,51]{1,0:T(8,128)S(1)} %copy-done.27), kind=kOutput, calls=%fused_computation.49 | convolution fusion | flops 5462304 | bytes 378624 | tf_op jit(solution)/shard_map/transpose(jvp(hqk,khd->qhd))/dot_general | solution.py:33
  96.2 0.6 fusion.58
  98.2 5.0 %fusion.77 = (f32[51]{0:T(128)S(1)}, f32[51,1024]{1,0:T(8,128)S(1)}) fusion(bf16[51,1024]{1,0:T(8,128)(2,1)S(1)} %gather_fusion.2, f32[51]{0:T(128)S(1)} %copy-done.20, bf16[51,3072]{1,0:T(8,128)(2,1)S(1)} %reshape.268, bf16[1024,3072]{1,0:T(8,128)(2,1)} %param.12), kind=kOutput, calls=%fused_computation.151 | convolution fusion | flops 321177536 | bytes 6918552 | tf_op jit(solution)/shard_map/transpose(jvp())/dot_general | solution.py:46
  103.7 10.8 %all-gather.1 = bf16[4,51,1024]{2,1,0:T(8,128)(2,1)S(1)} all-gather(bf16[1,51,1024]{2,1,0:T(8,128)(2,1)S(1)} %fusion.105), channel_id=1, replica_groups=mesh['dp'=8,'mask'=4] {'mask'}, dimensions={0}, use_global_device_ids=true | all-gather | bytes 522240 | tf_op jit(solution)/shard_map/all_gather | solution.py:134
  114.7 1.2 fusion.129
  (138 shorter events, 7.8 us)
Async XLA Ops:
  7.2 28.1 %copy-start = (bf16[1024,1024]{1,0:T(8,128)(2,1)S(1)}, bf16[1024,1024]{1,0:T(8,128)(2,1)}, u32[]{:S(2)}) copy-start(bf16[1024,1024]{1,0:T(8,128)(2,1)} %param.13) | copy-start | bytes 6291460
  7.2 65.1 %all-gather.4.cloned.1.call-start = ((), (), s32[]{:S(2)}) async-start(), calls=%async_computation.1 | async-start | bytes 2621440 | tf_op jit(solution)/shard_map/all_gather | solution.py:115
  33.4 3.0 %copy-start.17 = (bf16[64,768]{1,0:T(8,128)(2,1)S(1)}, bf16[64,768]{1,0:T(8,128)(2,1)}, u32[]{:S(2)}) copy-start(bf16[64,768]{1,0:T(8,128)(2,1)} %param.9) | copy-start | bytes 294916
  35.3 5.4 %copy-start.36 = (s32[4,51]{1,0:T(4,128)S(1)}, s32[4,51]{1,0:T(4,128)}, u32[]{:S(2)}) copy-start(s32[4,51]{1,0:T(4,128)} %param.10) | copy-start | bytes 2452
  37.3 33.3 %all-to-all-start = ((bf16[64,4,192]{2,0,1:T(8,128)(2,1)}), bf16[64,4,192]{2,0,1:T(8,128)(2,1)S(1)}, u32[]{:S(2)}, u32[]{:S(2)}) async-start(bf16[64,4,192]{2,0,1:T(8,128)(2,1)} %copy.73), calls=%async_computation | async-start | bytes 262144 | tf_op jit(solution)/shard_map/all_to_all | solution.py:128
  40.6 12.7 %copy-start.29 = (u32[51]{0:T(128)}, u32[51]{0:T(128)S(1)}, u32[]{:S(2)}) copy-start(u32[51]{0:T(128)S(1)} %iota_add_fusion) | copy-start | bytes 616
  41.3 9.8 %copy-start.28 = (s32[1024]{0:T(1024)}, s32[1024]{0:T(1024)S(1)}, u32[]{:S(2)}) copy-start(s32[1024]{0:T(1024)S(1)} %pad_clamp_fusion) | copy-start | bytes 12292
  42.2 0.5 copy-start.19
  42.4 4.7 %copy-start.39 = (f32[51]{0:T(128)}, f32[51]{0:T(128)S(1)}, u32[]{:S(2)}) copy-start(f32[51]{0:T(128)S(1)} %fusion.75) | copy-start | bytes 616
  42.7 4.4 %copy-start.31 = (f32[51]{0:T(128)}, f32[51]{0:T(128)S(1)}, u32[]{:S(2)}) copy-start(f32[51]{0:T(128)S(1)} %fusion.116) | copy-start | bytes 616
  47.6 0.7 copy-start.5
  47.6 1.2 copy-start.7
  47.6 1.2 copy-start.10
  48.8 0.6 copy-start.25
  48.8 0.9 copy-start.14
  49.8 2.7 %copy-start.37 = (bf16[1024]{0:T(1024)(128)(2,1)S(1)}, bf16[1024]{0:T(1024)(128)(2,1)}, u32[]{:S(2)}) copy-start(bf16[1024]{0:T(1024)(128)(2,1)} %param.14) | copy-start | bytes 6148
  53.4 2.2 %copy-start.1 = (bf16[256,1024]{1,0:T(8,128)(2,1)S(1)}, bf16[256,1024]{1,0:T(8,128)(2,1)}, u32[]{:S(2)}) copy-start(bf16[256,1024]{1,0:T(8,128)(2,1)} %compare_select_fusion) | copy-start | bytes 1572868
  54.5 0.6 copy-start.12
  65.5 3.8 %copy-start.35 = (s32[204,1]{0,1:T(1,128)S(1)}, s32[204,1]{0,1:T(1,128)}, u32[]{:S(2)}) copy-start(s32[204,1]{0,1:T(1,128)} %reshape.257) | copy-start | bytes 2452
  65.6 4.4 %copy-start.26 = (f32[16,51]{1,0:T(8,128)S(1)}, f32[16,51]{1,0:T(8,128)}, u32[]{:S(2)}) copy-start(f32[16,51]{1,0:T(8,128)} %copy-done.25) | copy-start | bytes 9796
  68.6 1.9 %copy-start.21 = (f32[256]{0:T(256)}, f32[256]{0:T(256)S(1)}, u32[]{:S(2)}) copy-start(f32[256]{0:T(256)S(1)} %broadcast_multiply_fusion.3) | copy-start | bytes 3076
  68.8 1.8 %copy-start.23 = (f32[256]{0:T(256)}, f32[256]{0:T(256)S(1)}, u32[]{:S(2)}) copy-start(f32[256]{0:T(256)S(1)} %fusion.39) | copy-start | bytes 3076
  70.6 4.2 %copy-start.2 = (f32[256,768]{1,0:T(8,128)S(1)}, f32[256,768]{1,0:T(8,128)}, u32[]{:S(2)}) copy-start(f32[256,768]{1,0:T(8,128)} %copy.83) | copy-start | bytes 2359300
  74.8 4.7 %copy-start.22 = (f32[256]{0:T(256)S(1)}, f32[256]{0:T(256)}, u32[]{:S(2)}) copy-start(f32[256]{0:T(256)} %copy-done.21) | copy-start | bytes 3076
  74.8 4.7 %copy-start.34 = (f32[256]{0:T(256)S(1)}, f32[256]{0:T(256)}, u32[]{:S(2)}) copy-start(f32[256]{0:T(256)} %fusion.114) | copy-start | bytes 3076
  74.8 4.7 %copy-start.38 = (f32[256]{0:T(256)S(1)}, f32[256]{0:T(256)}, u32[]{:S(2)}) copy-start(f32[256]{0:T(256)} %get-tuple-element.11) | copy-start | bytes 3076
  74.8 4.7 %copy-start.41 = (bf16[768,1024]{1,0:T(8,128)(2,1)S(1)}, bf16[768,1024]{1,0:T(8,128)(2,1)}, u32[]{:S(2)}) copy-start(bf16[768,1024]{1,0:T(8,128)(2,1)} %param.17) | copy-start | bytes 4718596
  79.5 3.5 %copy-start.24 = (f32[256]{0:T(256)S(1)}, f32[256]{0:T(256)}, u32[]{:S(2)}) copy-start(f32[256]{0:T(256)} %copy-done.23) | copy-start | bytes 3076
  83.0 2.6 %copy-start.9 = (bf16[256,768]{1,0:T(8,128)(2,1)}, bf16[256,768]{1,0:T(8,128)(2,1)S(1)}, u32[]{:S(2)}) copy-start(bf16[256,768]{1,0:T(8,128)(2,1)S(1)} %get-tuple-element.18) | copy-start | bytes 1179652
  85.6 3.2 %copy-start.3 = (bf16[3,16,48,48]{3,2,1,0:T(8,128)(2,1)S(1)}, bf16[3,16,48,48]{3,2,1,0:T(8,128)(2,1)}, u32[]{:S(2)}) copy-start(bf16[3,16,48,48]{3,2,1,0:T(8,128)(2,1)} %param.16) | copy-start | bytes 663556
  89.9 3.1 %copy-start.13 = (pred[51,1024]{1,0:T(8,128)(4,1)S(1)}, pred[51,1024]{1,0:T(8,128)(4,1)}, u32[]{:S(2)}) copy-start(pred[51,1024]{1,0:T(8,128)(4,1)} %copy-done.12) | copy-start | bytes 156676
  89.9 3.1 %copy-start.33 = (pred[51]{0:T(512)(128)(4,1)S(1)}, pred[51]{0:T(512)(128)(4,1)}, u32[]{:S(2)}) copy-start(pred[51]{0:T(512)(128)(4,1)} %get-tuple-element.4) | copy-start | bytes 157
  92.1 2.0 %copy-start.27 = (f32[16,51]{1,0:T(8,128)S(1)}, f32[16,51]{1,0:T(8,128)}, u32[]{:S(2)}) copy-start(f32[16,51]{1,0:T(8,128)} %copy-done.25) | copy-start | bytes 9796
  93.0 2.4 %copy-start.11 = (bf16[51,1,16,64]{3,2,1,0:T(8,128)(2,1)S(1)}, bf16[51,1,16,64]{3,2,1,0:T(8,128)(2,1)}, u32[]{:S(2)}) copy-start(bf16[51,1,16,64]{3,2,1,0:T(8,128)(2,1)} %copy-done.10) | copy-start | bytes 313348
  93.0 2.4 %copy-start.18 = (f32[16,51]{1,0:T(8,128)S(1)}, f32[16,51]{1,0:T(8,128)}, u32[]{:S(2)}) copy-start(f32[16,51]{1,0:T(8,128)} %multiply_divide_fusion) | copy-start | bytes 9796
  93.8 1.9 %copy-start.6 = (bf16[51,1,16,64]{3,2,1,0:T(8,128)(2,1)S(1)}, bf16[51,1,16,64]{3,2,1,0:T(8,128)(2,1)}, u32[]{:S(2)}) copy-start(bf16[51,1,16,64]{3,2,1,0:T(8,128)(2,1)} %copy-done.5) | copy-start | bytes 313348
  93.8 1.9 %copy-start.8 = (bf16[51,1,16,64]{3,2,1,0:T(8,128)(2,1)S(1)}, bf16[51,1,16,64]{3,2,1,0:T(8,128)(2,1)}, u32[]{:S(2)}) copy-start(bf16[51,1,16,64]{3,2,1,0:T(8,128)(2,1)} %copy-done.7) | copy-start | bytes 313348
  94.0 1.4 %copy-start.15 = (f32[16,51,51]{1,2,0:T(8,128)S(1)}, f32[16,51,51]{1,2,0:T(8,128)}, u32[]{:S(2)}) copy-start(f32[16,51,51]{1,2,0:T(8,128)} %copy-done.14) | copy-start | bytes 499396
  97.1 1.1 copy-start.20
  98.2 5.0 %copy-start.40 = (f32[51]{0:T(128)S(1)}, f32[51]{0:T(128)}, u32[]{:S(2)}) copy-start(f32[51]{0:T(128)} %copy-done.39) | copy-start | bytes 616
  98.2 5.0 %copy-start.32 = (f32[51]{0:T(128)S(1)}, f32[51]{0:T(128)}, u32[]{:S(2)}) copy-start(f32[51]{0:T(128)} %copy-done.31) | copy-start | bytes 616
  98.2 5.3 %copy-start.4 = (u32[51,1024]{1,0:T(8,128)S(1)}, u32[51,1024]{1,0:T(8,128)}, u32[]{:S(2)}) copy-start(u32[51,1024]{1,0:T(8,128)} %gather_fusion.1) | copy-start | bytes 626692
  98.2 5.3 %copy-start.30 = (u32[51]{0:T(128)S(1)}, u32[51]{0:T(128)}, u32[]{:S(2)}) copy-start(u32[51]{0:T(128)} %copy-done.29) | copy-start | bytes 616
  103.2 11.5 %copy-start.16 = (bf16[204,192]{1,0:T(8,128)(2,1)S(1)}, bf16[204,192]{1,0:T(8,128)(2,1)}, u32[]{:S(2)}) copy-start(bf16[204,192]{1,0:T(8,128)(2,1)} %gather_fusion) | copy-start | bytes 235012
Sparse Core Ops, SparseCore 0:
  36.6 35.5 all-gather.3
